TPU v7x, 256 devices: a whole 4x4x8 slice. The times are simulated.
256 devices in a mesh: seq: 32 (over x, z), tensor: 8 (over y, core).
Axes of the slice: x: 4, y: 4, z: 8, core: 2. Of those that a mesh axis runs over, the one named last changes fastest.
Arguments:
- queries: bfloat16 [10240, 4096], P('seq', 'tensor'), may hold values from -8 to 8
- key_rows: bfloat16 [10240, 1024], P('seq', 'tensor'), may hold values from -8 to 8
- value_rows: bfloat16 [10240, 1024], P('seq', 'tensor'), may hold values from -6 to 6
- out_weight: bfloat16 [4096, 8192], P('tensor', 'seq'), may hold values from -0.09375 to 0.09375
- residual_in: bfloat16 [10240, 8192], P('seq'), may hold values from -0.1796875 to 0.1796875
- norm_gain: bfloat16 [8192], replicated, may hold values from 0.099609375 to 1.8984375
- prompt_lengths: int32 [18], replicated, may hold values from 1 to 5120, 10240 in all
Outputs:
- normed: bfloat16 [10240, 8192], P('seq')
- cache_keys: bfloat16 [22528, 1024], P('seq', 'tensor')
- cache_values: bfloat16 [22528, 1024], P('seq', 'tensor')
Inputs may be any that keep to these rules, and one draw needn't show every extreme that they name: `prompt_lengths`: the 18 lengths sum to 10240, and the largest is 5120.
All inputs are finite; a program needn't handle non-finite values.
Results may differ from a plain program's by a relative error of at most 0.019.
Values may be sent and summed in bfloat16 or wider, within the bound.
No kernel may reach another device: no remote copies, remote signals or barrier semaphores. Data moves between devices by JAX's collectives and lax.ppermute only.
A program may use at most 192 MiB of HBM per device.

v0:
```python
import math

import jax
import jax.numpy as jnp
from jax import lax
from jax.sharding import PartitionSpec as P

HD = 128
PAGE = 128
SLOT_DEV = 704


def position_of(stored, per_device, devices):
    half_block = per_device // 2
    device = stored // per_device
    offset = stored % per_device
    return jnp.where(
        offset < half_block,
        device * half_block + offset,
        (2 * devices - 1 - device) * half_block + offset - half_block,
    )


def stored_row(position, per_device, devices):
    half_block = per_device // 2
    block_index = position // half_block
    device = jnp.where(block_index < devices, block_index, 2 * devices - 1 - block_index)
    offset = position % half_block + jnp.where(block_index < devices, 0, half_block)
    return device * per_device + offset


def segment_of(position, lengths):
    doc_ends = jnp.cumsum(lengths, dtype=jnp.int32)
    return jnp.sum(
        (position[:, None] >= doc_ends[None, :]).astype(jnp.int32), axis=1, dtype=jnp.int32
    )


def slot_source(slot_ids, lengths, page_size):
    padded = (lengths + page_size - 1) // page_size * page_size
    page_ends = jnp.cumsum(padded, dtype=jnp.int32)
    page_starts = page_ends - padded
    doc_ends = jnp.cumsum(lengths, dtype=jnp.int32)
    doc_starts = doc_ends - lengths
    prompt = jnp.sum(
        (slot_ids[:, None] >= page_ends[None, :]).astype(jnp.int32), axis=1, dtype=jnp.int32
    )
    clipped = jnp.minimum(prompt, lengths.shape[0] - 1)
    within = slot_ids - jnp.take(page_starts, clipped)
    is_live = (prompt < lengths.shape[0]) & (within < jnp.take(lengths, clipped))
    return (jnp.take(doc_starts, clipped) + within, is_live)


def body(queries, key_rows, value_rows, out_weight, residual_in, norm_gain, prompt_lengths):
    seq_count = lax.axis_size("seq")
    seq_index = lax.axis_index("seq")
    per_device = queries.shape[0]
    kv_local = key_rows.shape[1] // HD
    group_size = queries.shape[1] // (kv_local * HD)
    score_scale = 1.0 / math.sqrt(HD)
    local_rows = jnp.arange(per_device, dtype=jnp.int32) + seq_index * per_device
    my_position = position_of(local_rows, per_device, seq_count)
    my_segment = segment_of(my_position, prompt_lengths)
    grouped = queries.reshape(per_device, kv_local, group_size, HD)
    key_piece = lax.all_gather(key_rows, "seq", axis=0, tiled=True)
    value_piece = lax.all_gather(value_rows, "seq", axis=0, tiled=True)
    piece_rows = key_piece.shape[0]
    key_position = position_of(jnp.arange(piece_rows, dtype=jnp.int32), per_device, seq_count)
    key_segment = segment_of(key_position, prompt_lengths)
    allowed = (key_position[None, :] <= my_position[:, None]) & (
        key_segment[None, :] == my_segment[:, None]
    )
    top_old = jnp.full((kv_local, group_size, per_device), -1e30, jnp.float32)
    scores = (
        jnp.einsum(
            "qgjd,kgd->gjqk",
            grouped,
            key_piece.reshape(piece_rows, kv_local, HD),
            preferred_element_type=jnp.float32,
        )
        * score_scale
    )
    scores = jnp.where(allowed, scores, -1e30)
    top_new = jnp.maximum(top_old, jnp.max(scores, axis=-1))
    weights = jnp.where(allowed, jnp.exp(scores - top_new[..., None]), 0.0)
    total_new = jnp.sum(weights, axis=-1)
    accum_new = jnp.einsum(
        "gjqk,kgd->gjqd",
        weights.astype(jnp.bfloat16),
        value_piece.reshape(piece_rows, kv_local, HD),
        preferred_element_type=jnp.float32,
    )
    attended = jnp.transpose(accum_new / total_new[..., None], (2, 0, 1, 3))
    attended = attended.reshape(per_device, -1).astype(jnp.bfloat16)
    partial_value = jnp.dot(
        attended,
        lax.all_gather(out_weight, "seq", axis=1, tiled=True),
        preferred_element_type=jnp.float32,
    )
    projected = lax.psum(partial_value.astype(jnp.bfloat16), "tensor").astype(jnp.float32)
    hidden = residual_in.astype(jnp.float32) + projected
    mean_square = jnp.mean(hidden * hidden, axis=-1, keepdims=True)
    normed = (hidden * lax.rsqrt(mean_square + 1e-05) * norm_gain.astype(jnp.float32)).astype(
        jnp.bfloat16
    )
    slot_ids = seq_index * SLOT_DEV + jnp.arange(SLOT_DEV, dtype=jnp.int32)
    source, is_live = slot_source(slot_ids, prompt_lengths, PAGE)
    target = stored_row(source, per_device, seq_count)
    empty_cache = jnp.zeros((SLOT_DEV, kv_local * HD), jnp.bfloat16)
    key_piece = lax.all_gather(key_rows, "seq", axis=0, tiled=True)
    value_piece = lax.all_gather(value_rows, "seq", axis=0, tiled=True)
    piece_rows = key_piece.shape[0]
    found = is_live & (target >= 0) & (target < piece_rows)
    safe_index = jnp.clip(target, 0, piece_rows - 1)
    cache_keys = jnp.where(found[:, None], jnp.take(key_piece, safe_index, axis=0), empty_cache)
    cache_values = jnp.where(found[:, None], jnp.take(value_piece, safe_index, axis=0), empty_cache)
    return (normed, cache_keys, cache_values)


def solution(mesh):
    return jax.shard_map(
        body,
        mesh=mesh,
        in_specs=(
            P("seq", "tensor"),
            P("seq", "tensor"),
            P("seq", "tensor"),
            P("tensor", "seq"),
            P("seq", None),
            P(),
            P(),
        ),
        out_specs=(P("seq", None), P("seq", "tensor"), P("seq", "tensor")),
        check_vma=False,
    )
```

profile of v0, /device:TPU:1, one launch (start us, length us, event | category | flops | bytes accessed | tf_op | source)
XLA Modules:
  0.0 381.7 jit_solution(8324192015222926720)
XLA Ops:
  7.2 0.0 copy-start
  7.2 0.0 all-gather.4.cloned.1.call-start
  7.2 0.7 all-gather.4.cloned.1.call-update
  7.9 0.0 all-gather.6.cloned.1.call-start
  8.0 0.7 all-gather.6.cloned.1.call-update
  8.7 0.0 all-gather.8.cloned.1.call-start
  8.7 0.7 all-gather.8.cloned.1.call-update
  9.4 0.0 all-reduce.2.cloned.1.call-start
  9.4 0.7 copy.17
  10.2 0.1 reduce.2
  10.4 0.1 convert_reduce_fusion.2
  10.5 0.2 convert_reduce_fusion
  10.8 4.6 %compare_and_fusion = pred[320,10240]{1,0:T(8,128)(4,1)} fusion(s32[10240]{0:T(1024)S(1)} %convert_reduce_fusion, s32[10240]{0:T(1024)S(1)} %fusion.38, s32[320]{0:T(512)S(1)} %convert_reduce_fusion.2, s32[320]{0:T(512)S(1)} %add_select_fusion.5), kind=kLoop, calls=%fused_computation.10 | loop fusion | flops 9830400 | bytes 3361280 | tf_op jit(solution)/shard_map/and | solution.py:70
  15.3 74.5 %all-gather.4.cloned.1.call-done = bf16[10240,128]{1,0:T(8,128)(2,1)} async-done(((bf16[320,128]{1,0:T(8,128)(2,1)}), bf16[10240,128]{1,0:T(8,128)(2,1)}) %all-gather.4.cloned.1.call-update) | async-done | bytes 2621456 | tf_op jit(solution)/shard_map/all_gather | solution.py:65
  89.8 0.0 copy-done
  89.8 22.6 %fusion = (f32[4,320]{1,0:T(4,128)S(1)}, f32[10240,320,4]{0,1,2:T(8,128)}) fusion(pred[320,10240]{1,0:T(8,128)(4,1)} %compare_and_fusion, bf16[10240,128]{1,0:T(8,128)(2,1)} %all-gather.4.cloned.1.call-done, bf16[320,512]{1,0:T(8,128)(2,1)S(1)} %copy-done), kind=kOutput, calls=%fused_computation.4 | convolution fusion | flops 3394763520 | bytes 58659840 | tf_op jit(solution)/shard_map/qgjd,kgd->gjqk/dot_general | solution.py:75
  112.4 22.7 %fusion.1 = f32[4,320]{1,0:T(4,128)S(1)} fusion(f32[10240,320,4]{0,1,2:T(8,128)} %get-tuple-element.66, f32[4,320]{1,0:T(4,128)S(1)} %broadcast_maximum_fusion, pred[320,10240]{1,0:T(8,128)(4,1)} %compare_and_fusion), kind=kLoop, calls=%fused_computation.5 | loop fusion | flops 65534720 | bytes 55715840 | tf_op jit(solution)/shard_map/reduce_sum | solution.py:86
  135.1 33.1 %all-gather.6.cloned.1.call-done = bf16[10240,128]{1,0:T(8,128)(2,1)} async-done(((bf16[320,128]{1,0:T(8,128)(2,1)}), bf16[10240,128]{1,0:T(8,128)(2,1)}) %all-gather.6.cloned.1.call-update) | async-done | bytes 2621456 | tf_op jit(solution)/shard_map/all_gather | solution.py:66
  168.2 23.3 %fusion.20 = bf16[320,1,4,128]{3,0,2,1:T(8,128)(2,1)S(1)} fusion(bf16[10240,128]{1,0:T(8,128)(2,1)} %all-gather.6.cloned.1.call-done, f32[10240,320,4]{0,1,2:T(8,128)} %get-tuple-element.66, f32[4,320]{1,0:T(4,128)S(1)} %broadcast_maximum_fusion, pred[320,10240]{1,0:T(8,128)(4,1)} %compare_and_fusion, f32[4,320]{1,0:T(4,128)S(1)} %fusion.1), kind=kOutput, calls=%fused_computation.20 | convolution fusion | flops 3421306880 | bytes 58664960 | tf_op jit(solution)/shard_map/gjqk,kgd->gjqd/dot_general | solution.py:87
  191.6 0.3 copy.19
  191.9 0.0 copy-start.4
  191.9 0.0 copy-start.5
  191.9 80.5 %all-gather.8.cloned.1.call-done = bf16[512,8192]{1,0:T(8,128)(2,1)} async-done(((bf16[512,256]{1,0:T(8,128)(2,1)}), bf16[512,8192]{1,0:T(8,128)(2,1)}) %all-gather.8.cloned.1.call-update) | async-done | bytes 8388624 | tf_op jit(solution)/shard_map/all_gather | solution.py:97
  272.4 0.0 copy-start.3
  272.4 8.1 %convolution_convert_fusion = bf16[320,8192]{1,0:T(8,128)(2,1)} fusion(bf16[512,8192]{1,0:T(8,128)(2,1)} %all-gather.8.cloned.1.call-done, bf16[40,8,4,128]{3,2,1,0:T(4,128)(2,1)S(1)} %bitcast.120), kind=kOutput, calls=%fused_computation.11 | convolution fusion | flops 2686976000 | bytes 13959168 | tf_op jit(solution)/shard_map/dot_general | solution.py:95
  280.5 0.0 all-reduce.2.cloned.1.call-update
  280.5 0.0 copy-done.4
  280.6 0.1 copy.20
  280.7 0.1 reduce.3
  280.8 0.0 copy-done.5
  280.9 0.7 fusion.58
  281.6 0.7 fusion.57
  282.3 0.7 fusion.55
  283.1 0.1 convert_reduce_fusion.1
  283.1 33.8 %compare_and_fusion.3 = (pred[704]{0:T(1024)(128)(4,1)S(1)}, s32[704]{0:T(1024)S(1)}) fusion(s32[704]{0:T(1024)S(1)} %convert_reduce_fusion.1, s32[]{:T(128)} %bitcast.44, s32[]{:T(128)} %bitcast.43, s32[]{:T(128)} %bitcast.42, s32[]{:T(128)} %bitcast.41, s32[]{:T(128)} %bitcast.40, s32[]{:T(128)} %bitcast.39, s32[]{:T(128)} %bitcast.38, s32[]{:T(128)} %bitcast.37, ...), kind=kLoop, calls=%fused_computation.64 | loop fusion | flops 75328 | bytes 6556 | tf_op jit(solution)/shard_map/and | solution.py:113
  317.0 0.0 copy-done.3
  317.0 2.0 gather_fusion
  319.0 3.9 %gather_fusion.1 = bf16[704,128]{1,0:T(8,128)(2,1)S(1)} fusion(bf16[10240,128]{1,0:T(8,128)(2,1)} %all-gather.6.cloned.1.call-done, s32[1024]{0:T(1024)S(1)} %pad_clamp_fusion), kind=kCustom, calls=%fused_computation.1.clone | custom fusion | bytes 363264 | tf_op jit(solution)/shard_map/jit(_take)/gather | solution.py:116
  322.9 1.0 select_select_fusion
  323.9 38.1 %all-reduce.2.cloned.1.call-done = bf16[320,8192]{1,0:T(8,128)(2,1)} async-done(((bf16[320,8192]{1,0:T(8,128)(2,1)}), bf16[320,8192]{1,0:T(8,128)(2,1)}) %all-reduce.2.cloned.1.call-update) | async-done | bytes 5242896 | tf_op jit(solution)/shard_map/psum | solution.py:100
  362.0 0.0 copy-start.2
  362.0 0.0 copy-start.1
  362.0 6.0 %multiply_reduce_fusion = f32[320]{0:T(512)S(1)} fusion(bf16[320,8192]{1,0:T(8,128)(2,1)} %all-reduce.2.cloned.1.call-done, bf16[320,8192]{1,0:T(8,128)(2,1)} %param.15), kind=kLoop, calls=%fused_computation.13 | loop fusion | flops 13106880 | bytes 10487040 | tf_op jit(solution)/shard_map/reduce_sum | solution.py:102
  368.0 0.0 copy-done.2
  368.0 7.1 %multiply_convert_fusion = bf16[320,8192]{1,0:T(8,128)(2,1)} fusion(bf16[320,8192]{1,0:T(8,128)(2,1)S(1)} %copy-done.2, bf16[320,8192]{1,0:T(8,128)(2,1)} %param.15, f32[8192]{0:T(1024)S(1)} %convert_element_type.49, f32[320]{0:T(512)S(1)} %add_rsqrt_fusion), kind=kLoop, calls=%fused_computation.12 | loop fusion | flops 15728640 | bytes 15762688 | tf_op jit(solution)/shard_map/convert_element_type | solution.py:103
  375.2 0.0 copy-done.1
  (13 shorter events, 0.2 us)
Async XLA Ops:
  7.2 82.6 %copy-start = (bf16[320,512]{1,0:T(8,128)(2,1)S(1)}, bf16[320,512]{1,0:T(8,128)(2,1)}, u32[]{:S(2)}) copy-start(bf16[320,512]{1,0:T(8,128)(2,1)} %param.11) | copy-start | bytes 983044
  7.2 82.6 %all-gather.4.cloned.1.call-start = ((), (), s32[]{:S(2)}) async-start(), calls=%async_computation | async-start | bytes 2703360 | tf_op jit(solution)/shard_map/all_gather | solution.py:65
  7.9 160.3 %all-gather.6.cloned.1.call-start = ((), (), s32[]{:S(2)}) async-start(), calls=%async_computation.1 | async-start | bytes 2703360 | tf_op jit(solution)/shard_map/all_gather | solution.py:66
  8.7 263.7 %all-gather.8.cloned.1.call-start = ((), (), s32[]{:S(2)}) async-start(), calls=%async_computation.2 | async-start | bytes 8650752 | tf_op jit(solution)/shard_map/all_gather | solution.py:97
  9.4 352.6 %all-reduce.2.cloned.1.call-start = ((), (), s32[]{:S(2)}) async-start(), calls=%async_computation.3 | async-start | bytes 10485760 | tf_op jit(solution)/shard_map/psum | solution.py:100
  191.9 88.7 %copy-start.4 = (s32[18]{0:T(128)S(1)}, s32[18]{0:T(128)}, u32[]{:S(2)}) copy-start(s32[18]{0:T(128)} %param.17) | copy-start | bytes 220
  191.9 89.0 %copy-start.5 = (bf16[8192]{0:T(1024)(128)(2,1)S(1)}, bf16[8192]{0:T(1024)(128)(2,1)}, u32[]{:S(2)}) copy-start(bf16[8192]{0:T(1024)(128)(2,1)} %param.16) | copy-start | bytes 49156
  272.4 44.6 %copy-start.3 = (bf16[10240,128]{1,0:T(8,128)(2,1)S(1)}, bf16[10240,128]{1,0:T(8,128)(2,1)}, u32[]{:S(2)}) copy-start(bf16[10240,128]{1,0:T(8,128)(2,1)} %all-gather.4.cloned.1.call-done) | copy-start | bytes 7864324
  362.0 6.0 %copy-start.2 = (bf16[320,8192]{1,0:T(8,128)(2,1)S(1)}, bf16[320,8192]{1,0:T(8,128)(2,1)}, u32[]{:S(2)}) copy-start(bf16[320,8192]{1,0:T(8,128)(2,1)} %all-reduce.2.cloned.1.call-done) | copy-start | bytes 15728644
  362.0 13.1 %copy-start.1 = (bf16[320,512]{1,0:T(8,128)(2,1)S(1)}, bf16[320,512]{1,0:T(8,128)(2,1)}, u32[]{:S(2)}) copy-start(bf16[320,512]{1,0:T(8,128)(2,1)} %param.11) | copy-start | bytes 983044
Sparse Core Ops, SparseCore 0:
  10.6 79.1 all-gather.3
  92.4 75.8 all-gather.5
  170.7 101.6 all-gather.7
  280.7 81.3 all-reduce.1
where the time goes:
time: 382 us
  waiting for transfers between devices  228 us (60%)
  other arithmetic  76 us (20%)
  matrix products  54.1 us (14%)
  between operations  13.9 us (4%)
  local copies, waits for them, and re-layouts  9.23 us (2%)
    all_gather x1, waiting for transfers between devices, body(): lax.all_gather(out_weight, 'seq', axis=1, tiled=True)  80.5 us
    all_gather x1, waiting for transfers between devices, body(): key_piece = lax.all_gather(key_rows, 'seq', axis=0, tiled=True)  74.5 us
    psum x1, waiting for transfers between devices, body(): lax.psum(partial_value.astype(jnp.bfloat16), 'tensor').astype(jnp.float32)  38.1 us
    and x1, other arithmetic, body(): found = is_live & (target >= 0) & (target < piece_rows)  33.8 us
    all_gather x1, waiting for transfers between devices, body(): value_piece = lax.all_gather(value_rows, 'seq', axis=0, tiled=True)  33.1 us
    dot_general x1, matrix products, body(): jnp.einsum('gjqk,kgd->gjqd', weights.astype(jnp.bfloat16), value_piece.re...  23.3 us
    reduce_sum x1, other arithmetic, body(): total_new = jnp.sum(weights, axis=-1)  22.7 us
    dot_general x1, matrix products, body(): jnp.einsum('qgjd,kgd->gjqk', grouped, key_piece.reshape(piece_rows, kv_lo...  22.6 us
  transfers between devices with their start and end apart: 4, of which 4 were waited for; matrix products, arithmetic and copies ran while one was open for 31% of the time, Pallas kernels for 0%

commit v1 on v0

--- a/solution.py
+++ b/solution.py
@@ -42,13 +42,14 @@
     page_starts = page_ends - padded
     doc_ends = jnp.cumsum(lengths, dtype=jnp.int32)
     doc_starts = doc_ends - lengths
-    prompt = jnp.sum(
-        (slot_ids[:, None] >= page_ends[None, :]).astype(jnp.int32), axis=1, dtype=jnp.int32
-    )
-    clipped = jnp.minimum(prompt, lengths.shape[0] - 1)
-    within = slot_ids - jnp.take(page_starts, clipped)
-    is_live = (prompt < lengths.shape[0]) & (within < jnp.take(lengths, clipped))
-    return (jnp.take(doc_starts, clipped) + within, is_live)
+    before = (slot_ids[:, None] >= page_ends[None, :]).astype(jnp.int32)
+    inside = (slot_ids[:, None] >= page_starts[None, :]).astype(jnp.int32) - before
+    page_start = jnp.sum(before * padded[None, :], axis=1, dtype=jnp.int32)
+    doc_start = jnp.sum(before * lengths[None, :], axis=1, dtype=jnp.int32)
+    length = jnp.sum(inside * lengths[None, :], axis=1, dtype=jnp.int32)
+    within = slot_ids - page_start
+    is_live = within < length
+    return (doc_start + within, is_live)
 
 
 def body(queries, key_rows, value_rows, out_weight, residual_in, norm_gain, prompt_lengths):
@@ -62,8 +63,12 @@
     my_position = position_of(local_rows, per_device, seq_count)
     my_segment = segment_of(my_position, prompt_lengths)
     grouped = queries.reshape(per_device, kv_local, group_size, HD)
-    key_piece = lax.all_gather(key_rows, "seq", axis=0, tiled=True)
-    value_piece = lax.all_gather(value_rows, "seq", axis=0, tiled=True)
+    kv_width = key_rows.shape[1]
+    kv_piece = lax.all_gather(
+        jnp.concatenate([key_rows, value_rows], axis=1), "seq", axis=0, tiled=True
+    )
+    key_piece = kv_piece[:, :kv_width]
+    value_piece = kv_piece[:, kv_width:]
     piece_rows = key_piece.shape[0]
     key_position = position_of(jnp.arange(piece_rows, dtype=jnp.int32), per_device, seq_count)
     key_segment = segment_of(key_position, prompt_lengths)
@@ -107,9 +112,6 @@
     source, is_live = slot_source(slot_ids, prompt_lengths, PAGE)
     target = stored_row(source, per_device, seq_count)
     empty_cache = jnp.zeros((SLOT_DEV, kv_local * HD), jnp.bfloat16)
-    key_piece = lax.all_gather(key_rows, "seq", axis=0, tiled=True)
-    value_piece = lax.all_gather(value_rows, "seq", axis=0, tiled=True)
-    piece_rows = key_piece.shape[0]
     found = is_live & (target >= 0) & (target < piece_rows)
     safe_index = jnp.clip(target, 0, piece_rows - 1)
     cache_keys = jnp.where(found[:, None], jnp.take(key_piece, safe_index, axis=0), empty_cache)

time: 382 us -> 310 us (0.81)
  waiting for transfers between devices: 228 us -> 184 us
  other arithmetic: 76 us -> 47.3 us
    all_gather x1, waiting for transfers between devices: 80.5 us -> 34.2 us  [body(): lax.all_gather(out_weight, 'seq', axis=1, tiled=True)]
    and x1, other arithmetic: 33.8 us -> 0.03 us  [body(): found = is_live & (target >= 0) & (target < piece_rows)]
    psum x1, waiting for transfers between devices: 38.1 us -> 71 us  [body(): lax.psum(partial_value.astype(jnp.bfloat16), 'tensor').astype(jnp.float32)]
    all_gather x2 -> x1, waiting for transfers between devices: 108 us -> 78.3 us  [body(): lax.all_gather(jnp.concatenate([key_rows, value_rows], axis=1), 'seq', ax...]
  transfers between devices with their start and end apart: 4 -> 3, of which waited for: 4 -> 3; matrix products, arithmetic and copies ran while one was open for 31% -> 29% of each run, Pallas kernels for 0% -> 0%
where the time goes in v1:
time: 310 us
  waiting for transfers between devices  184 us (59%)
  matrix products  54.1 us (17%)
  other arithmetic  47.3 us (15%)
  between operations  13.9 us (4%)
  local copies, waits for them, and re-layouts  10.7 us (3%)
    all_gather x1, waiting for transfers between devices, body(): lax.all_gather(jnp.concatenate([key_rows, value_rows], axis=1), 'seq', ax...  78.3 us
    psum x1, waiting for transfers between devices, body(): lax.psum(partial_value.astype(jnp.bfloat16), 'tensor').astype(jnp.float32)  71 us
    all_gather x1, waiting for transfers between devices, body(): lax.all_gather(out_weight, 'seq', axis=1, tiled=True)  34.2 us
    dot_general x1, matrix products, body(): jnp.einsum('gjqk,kgd->gjqd', weights.astype(jnp.bfloat16), value_piece.re...  23.2 us
    dot_general x1, matrix products, body(): jnp.einsum('qgjd,kgd->gjqk', grouped, key_piece.reshape(piece_rows, kv_lo...  22.9 us
    reduce_sum x1, other arithmetic, body(): total_new = jnp.sum(weights, axis=-1)  22.7 us
    dot_general x1, matrix products, body(): jnp.dot(attended, lax.all_gather(out_weight, 'seq', axis=1, tiled=True),...  7.96 us
    convert_element_type x1, other arithmetic, body(): (hidden * lax.rsqrt(mean_square + 1e-05) * norm_gain.astype(jnp.float32))...  7.13 us
  transfers between devices with their start and end apart: 3, of which 3 were waited for; matrix products, arithmetic and copies ran while one was open for 29% of the time, Pallas kernels for 0%

profile of v1, /device:TPU:1, one launch (start us, length us, event | category | flops | bytes accessed | tf_op | source)
XLA Modules:
  0.0 310.1 jit_solution(13555092218789178911)
XLA Ops:
  7.2 0.0 copy-start
  7.2 0.0 all-gather.3.cloned.1.call-start
  7.2 1.6 pad_maximum_fusion
  8.9 0.0 all-gather.3.cloned.1.call-update
  8.9 0.0 all-gather.5.cloned.1.call-start
  9.0 0.7 all-gather.5.cloned.1.call-update
  9.7 0.0 all-reduce.2.cloned.1.call-start
  9.7 0.7 copy.17
  10.5 0.1 reduce.2
  10.6 0.7 convert_element_type.52
  11.3 0.7 fusion.65
  12.0 0.1 copy.20
  12.1 0.1 reduce.3
  12.3 0.7 fusion.55
  13.0 0.7 fusion.64
  13.6 0.8 fusion.36
  14.5 0.1 convert_reduce_fusion.1
  14.6 0.2 convert_reduce_fusion
  14.8 4.6 %compare_and_fusion = pred[320,10240]{1,0:T(8,128)(4,1)} fusion(s32[10240]{0:T(1024)S(1)} %convert_reduce_fusion, s32[10240]{0:T(1024)S(1)} %fusion.43, s32[320]{0:T(512)S(1)} %convert_reduce_fusion.1, s32[320]{0:T(512)S(1)} %add_select_fusion.5), kind=kLoop, calls=%fused_computation.10 | loop fusion | flops 9830400 | bytes 3361280 | tf_op jit(solution)/shard_map/and | solution.py:75
  19.4 78.3 %all-gather.3.cloned.1.call-done = bf16[10240,256]{1,0:T(8,128)(2,1)} async-done(((bf16[320,256]{1,0:T(8,128)(2,1)}), bf16[10240,256]{1,0:T(8,128)(2,1)}) %all-gather.3.cloned.1.call-update) | async-done | bytes 5242896 | tf_op jit(solution)/shard_map/all_gather | solution.py:67
  97.7 0.0 copy-done
  97.7 22.9 %fusion = (f32[4,320]{1,0:T(4,128)S(1)}, f32[10240,320,4]{0,1,2:T(8,128)}) fusion(pred[320,10240]{1,0:T(8,128)(4,1)} %compare_and_fusion, bf16[10240,256]{1,0:T(8,128)(2,1)} %all-gather.3.cloned.1.call-done, bf16[320,512]{1,0:T(8,128)(2,1)S(1)} %copy-done), kind=kOutput, calls=%fused_computation.4 | convolution fusion | flops 3394763520 | bytes 58659840 | tf_op jit(solution)/shard_map/qgjd,kgd->gjqk/dot_general | solution.py:80
  120.5 22.7 %fusion.1 = f32[4,320]{1,0:T(4,128)S(1)} fusion(f32[10240,320,4]{0,1,2:T(8,128)} %get-tuple-element.14, f32[4,320]{1,0:T(4,128)S(1)} %broadcast_maximum_fusion, pred[320,10240]{1,0:T(8,128)(4,1)} %compare_and_fusion), kind=kLoop, calls=%fused_computation.5 | loop fusion | flops 65534720 | bytes 55715840 | tf_op jit(solution)/shard_map/reduce_sum | solution.py:91
  143.3 23.2 %fusion.20 = bf16[320,1,4,128]{3,0,2,1:T(8,128)(2,1)S(1)} fusion(f32[10240,320,4]{0,1,2:T(8,128)} %get-tuple-element.14, f32[4,320]{1,0:T(4,128)S(1)} %broadcast_maximum_fusion, pred[320,10240]{1,0:T(8,128)(4,1)} %compare_and_fusion, f32[4,320]{1,0:T(4,128)S(1)} %fusion.1, bf16[10240,256]{1,0:T(8,128)(2,1)} %all-gather.3.cloned.1.call-done), kind=kOutput, calls=%fused_computation.20 | convolution fusion | flops 3421306880 | bytes 58664960 | tf_op jit(solution)/shard_map/gjqk,kgd->gjqd/dot_general | solution.py:92
  166.5 0.3 copy.19
  166.8 34.2 %all-gather.5.cloned.1.call-done = bf16[512,8192]{1,0:T(8,128)(2,1)} async-done(((bf16[512,256]{1,0:T(8,128)(2,1)}), bf16[512,8192]{1,0:T(8,128)(2,1)}) %all-gather.5.cloned.1.call-update) | async-done | bytes 8388624 | tf_op jit(solution)/shard_map/all_gather | solution.py:102
  200.9 8.0 %convolution_convert_fusion = bf16[320,8192]{1,0:T(8,128)(2,1)} fusion(bf16[512,8192]{1,0:T(8,128)(2,1)} %all-gather.5.cloned.1.call-done, bf16[40,8,4,128]{3,2,1,0:T(4,128)(2,1)S(1)} %bitcast.67), kind=kOutput, calls=%fused_computation.11 | convolution fusion | flops 2686976000 | bytes 13959168 | tf_op jit(solution)/shard_map/dot_general | solution.py:100
  208.9 0.0 all-reduce.2.cloned.1.call-update
  208.9 3.7 %fusion.62 = (bf16[10240,128]{1,0:T(8,128)(2,1)S(1)}, bf16[10240,128]{1,0:T(8,128)(2,1)}) fusion(bf16[10240,256]{1,0:T(8,128)(2,1)} %all-gather.3.cloned.1.call-done), kind=kLoop, calls=%fused_computation.91 | loop fusion | bytes 10485760 | tf_op jit(solution)/shard_map/slice | solution.py:71
  212.6 3.8 %gather_fusion = bf16[704,128]{1,0:T(8,128)(2,1)S(1)} fusion(bf16[10240,128]{1,0:T(8,128)(2,1)} %get-tuple-element.10, s32[1024]{0:T(1024)S(1)} %pad_clamp_fusion), kind=kCustom, calls=%fused_computation.clone | custom fusion | bytes 363264 | tf_op jit(solution)/shard_map/jit(_take)/gather | solution.py:117
  216.5 2.0 gather_fusion.1
  218.5 1.0 select_select_fusion
  219.5 71.0 %all-reduce.2.cloned.1.call-done = bf16[320,8192]{1,0:T(8,128)(2,1)} async-done(((bf16[320,8192]{1,0:T(8,128)(2,1)}), bf16[320,8192]{1,0:T(8,128)(2,1)}) %all-reduce.2.cloned.1.call-update) | async-done | bytes 5242896 | tf_op jit(solution)/shard_map/psum | solution.py:105
  290.5 0.0 copy-start.2
  290.5 0.0 copy-start.1
  290.5 6.0 %multiply_reduce_fusion = f32[320]{0:T(512)S(1)} fusion(bf16[320,8192]{1,0:T(8,128)(2,1)} %all-reduce.2.cloned.1.call-done, bf16[320,8192]{1,0:T(8,128)(2,1)} %param.13), kind=kLoop, calls=%fused_computation.13 | loop fusion | flops 13106880 | bytes 10487040 | tf_op jit(solution)/shard_map/reduce_sum | solution.py:107
  296.5 0.0 copy-done.2
  296.5 7.1 %multiply_convert_fusion = bf16[320,8192]{1,0:T(8,128)(2,1)} fusion(bf16[320,8192]{1,0:T(8,128)(2,1)S(1)} %copy-done.2, bf16[320,8192]{1,0:T(8,128)(2,1)} %param.13, f32[8192]{0:T(1024)S(1)} %convert_element_type.52, f32[320]{0:T(512)S(1)} %add_rsqrt_fusion), kind=kLoop, calls=%fused_computation.12 | loop fusion | flops 15728640 | bytes 15762688 | tf_op jit(solution)/shard_map/convert_element_type | solution.py:108
  303.6 0.0 copy-done.1
  (11 shorter events, 0.2 us)
Async XLA Ops:
  7.2 90.5 %copy-start = (bf16[320,512]{1,0:T(8,128)(2,1)S(1)}, bf16[320,512]{1,0:T(8,128)(2,1)}, u32[]{:S(2)}) copy-start(bf16[320,512]{1,0:T(8,128)(2,1)} %param.9) | copy-start | bytes 983044
  7.2 90.5 %all-gather.3.cloned.1.call-start = ((), (), s32[]{:S(2)}) async-start(), calls=%async_computation | async-start | bytes 5406720 | tf_op jit(solution)/shard_map/all_gather | solution.py:67
  8.9 192.0 %all-gather.5.cloned.1.call-start = ((), (), s32[]{:S(2)}) async-start(), calls=%async_computation.1 | async-start | bytes 8650752 | tf_op jit(solution)/shard_map/all_gather | solution.py:102
  9.7 280.8 %all-reduce.2.cloned.1.call-start = ((), (), s32[]{:S(2)}) async-start(), calls=%async_computation.2 | async-start | bytes 10485760 | tf_op jit(solution)/shard_map/psum | solution.py:105
  290.5 6.0 %copy-start.2 = (bf16[320,8192]{1,0:T(8,128)(2,1)S(1)}, bf16[320,8192]{1,0:T(8,128)(2,1)}, u32[]{:S(2)}) copy-start(bf16[320,8192]{1,0:T(8,128)(2,1)} %all-reduce.2.cloned.1.call-done) | copy-start | bytes 15728644
  290.5 13.1 %copy-start.1 = (bf16[320,512]{1,0:T(8,128)(2,1)S(1)}, bf16[320,512]{1,0:T(8,128)(2,1)}, u32[]{:S(2)}) copy-start(bf16[320,512]{1,0:T(8,128)(2,1)} %param.9) | copy-start | bytes 983044
Sparse Core Ops, SparseCore 0:
  11.2 86.4 all-gather.2
  100.1 100.7 all-gather.4
  209.0 81.3 all-reduce.1
